TPU v7x, 32 devices: a whole 2x2x4 slice. The times are simulated.
32 devices in a mesh: grid: 8 (over y, x, core), band: 4 (over z).
Axes of the slice: x: 2, y: 2, z: 4, core: 2. Of those that a mesh axis runs over, the one named last changes fastest.
Arguments:
- occupied: bfloat16 [1024, 32, 24, 128], P('band', 'grid'), may hold values from -6 to 6
- potential: float32 [32, 24, 128], P('grid'), may hold values from 0.2 to 4
- shifts: float32 [64], P('band'), may hold values from 0.5 to 4
- source_term: float32 [64, 32, 24, 128], P('band', 'grid'), may hold values from -125 to 125
Outputs:
- solution: float32 [64, 32, 24, 128], P('band', 'grid')
- residual: float32 [64, 32, 24, 128], P('band', 'grid')
All inputs are finite; a program needn't handle non-finite values.
Results may differ from a plain program's by a relative error of at most 0.022.
Values may be sent and summed in bfloat16 or wider, within the bound.
No kernel may reach another device: no remote copies, remote signals or barrier semaphores. Data moves between devices by JAX's collectives and lax.ppermute only.
A program may use at most 128 MiB of HBM per device.

v0:
```python
import math
import jax
import jax.numpy as jnp
from jax import lax
from jax.sharding import PartitionSpec as P

ITERS = 2
COEFFICIENTS = (-205.0 / 72.0, 8.0 / 5.0, -1.0 / 5.0, 8.0 / 315.0, -1.0 / 560.0)


def with_halo(shard, sides, width):
    for axis, dim in sides:
        peers, length = (lax.axis_size(axis), shard.shape[dim])
        up = [(i, (i + 1) % peers) for i in range(peers - 1)]
        down = [(j, i) for i, j in up]
        last = lax.slice_in_dim(shard, length - width, length, axis=dim)
        leading = lax.slice_in_dim(shard, 0, width, axis=dim)
        before = lax.ppermute(last, axis, up)
        after = lax.ppermute(leading, axis, down)
        shard = jnp.concatenate([before, shard, after], axis=dim)
    return shard


def second_sum(padded, extent_x, extent_y, extent_z):
    middle = padded[:, 4 : 4 + extent_x, 4 : 4 + extent_y, 4 : 4 + extent_z]
    summed = 3.0 * COEFFICIENTS[0] * middle
    for offset in range(1, 5):
        along_x = (
            padded[:, 4 + offset : 4 + offset + extent_x, 4 : 4 + extent_y, 4 : 4 + extent_z]
            + padded[:, 4 - offset : 4 - offset + extent_x, 4 : 4 + extent_y, 4 : 4 + extent_z]
        )
        along_y = (
            padded[:, 4 : 4 + extent_x, 4 + offset : 4 + offset + extent_y, 4 : 4 + extent_z]
            + padded[:, 4 : 4 + extent_x, 4 - offset : 4 - offset + extent_y, 4 : 4 + extent_z]
        )
        along_z = (
            padded[:, 4 : 4 + extent_x, 4 : 4 + extent_y, 4 + offset : 4 + offset + extent_z]
            + padded[:, 4 : 4 + extent_x, 4 : 4 + extent_y, 4 - offset : 4 - offset + extent_z]
        )
        summed = (
            summed
            + COEFFICIENTS[offset] * along_x
            + COEFFICIENTS[offset] * along_y
            + COEFFICIENTS[offset] * along_z
        )
    return summed


def inner_product(first_field, second_field):
    return jnp.sum(first_field * second_field, axis=(1, 2, 3))


def expand(vector):
    return vector[:, None, None, None]


def body(occupied, potential, shifts, source_term):
    local_bands, width_x, width_y, width_z = source_term.shape
    local_occupied = occupied.shape[0]
    band_count = lax.axis_size("band")
    local_cells = width_x * width_y * width_z
    weight_scale = 2.0 / math.sqrt(
        local_occupied * band_count * local_cells * lax.axis_size("grid")
    )
    occupied_rows = occupied.reshape(local_occupied, local_cells)
    potential_shift = potential[None] + shifts[:, None, None, None]
    solution = jnp.zeros_like(source_term)
    residual = source_term
    direction = source_term
    norm_now = lax.psum(inner_product(source_term, source_term), "grid")
    for iteration in range(ITERS):
        padded = with_halo(direction.astype(jnp.bfloat16), (("grid", 1),), 4).astype(
            direction.dtype
        )
        padded = jnp.pad(padded, ((0, 0), (0, 0), (4, 4), (4, 4)))
        kinetic = -0.5 * second_sum(padded, width_x, width_y, width_z)
        rounded = direction.astype(jnp.bfloat16).reshape(local_bands, local_cells)
        partial_margin = lax.dot_general(
            occupied_rows,
            lax.all_gather(rounded, "band", axis=0, tiled=True),
            (((1,), (1,)), ((), ())),
            preferred_element_type=jnp.float32,
        )
        margins = lax.psum(partial_margin, "grid")
        scaled = (margins * weight_scale).astype(jnp.bfloat16)
        projected = lax.psum_scatter(
            lax.dot_general(
                scaled, occupied_rows, (((0,), (0,)), ((), ())), preferred_element_type=jnp.float32
            ).astype(jnp.bfloat16),
            "band",
            scatter_dimension=0,
            tiled=True,
        ).astype(jnp.float32)
        applied = kinetic + potential_shift * direction + projected.reshape(direction.shape)
        curvature = lax.psum(inner_product(direction, applied), "grid")
        step_size = norm_now / curvature
        solution = solution + expand(step_size) * direction
        residual = residual - expand(step_size) * applied
        if iteration + 1 < ITERS:
            norm_next = lax.psum(inner_product(residual, residual), "grid")
            direction = residual + expand(norm_next / norm_now) * direction
            norm_now = norm_next
    return (solution, residual)


def solution(mesh):
    in_specs = (
        P("band", "grid", None, None),
        P("grid", None, None),
        P("band"),
        P("band", "grid", None, None),
    )
    out_specs = (P("band", "grid", None, None), P("band", "grid", None, None))
    return jax.shard_map(body, mesh=mesh, in_specs=in_specs, out_specs=out_specs, check_vma=False)
```

profile of v0, /device:TPU:0, one launch (start us, length us, event | category | flops | bytes accessed | tf_op | source)
XLA Modules:
  0.0 345.8 jit_solution(5779249794180429042)
XLA Ops:
  7.2 1.2 convert_element_type.31
  8.4 0.9 copy.32
  9.4 40.6 %all-gather.3.cloned.1.call-done = bf16[64,12288]{1,0:T(8,128)(2,1)} async-done(((bf16[16,12288]{1,0:T(8,128)(2,1)}), bf16[64,12288]{1,0:T(8,128)(2,1)}) %all-gather.3.cloned.1.call-update) | async-done | bytes 1572880 | tf_op jit(solution)/shard_map/all_gather | solution.py:80
  50.0 5.8 %fusion.4 = f32[256,64]{1,0:T(8,128)} fusion(bf16[64,12288]{1,0:T(8,128)(2,1)} %all-gather.3.cloned.1.call-done, bf16[32,8,96,128]{3,2,1,0:T(8,128)(2,1)} %bitcast.35), kind=kOutput, calls=%fused_computation.38 | convolution fusion | flops 402653184 | bytes 7929856 | tf_op jit(solution)/shard_map/dot_general | solution.py:78
  55.9 51.9 %all-reduce.6.cloned.1.call-done = f32[256,64]{1,0:T(8,128)} async-done(((f32[256,64]{1,0:T(8,128)}), f32[256,64]{1,0:T(8,128)}) %all-reduce.6.cloned.1.call-update) | async-done | bytes 65552 | tf_op jit(solution)/shard_map/psum | solution.py:84
  107.8 6.2 %convolution_convert_fusion.1 = bf16[64,12288]{1,0:T(8,128)(2,1)} fusion(bf16[32,8,96,128]{3,2,1,0:T(8,128)(2,1)} %bitcast.36, f32[256,64]{1,0:T(8,128)} %all-reduce.6.cloned.1.call-done), kind=kOutput, calls=%fused_computation.33 | convolution fusion | flops 403472384 | bytes 7929856 | tf_op jit(solution)/shard_map/dot_general | solution.py:87
  114.0 1.4 collective-permute-start.1
  115.5 3.1 collective-permute-start
  118.5 1.3 collective-permute-done
  119.8 0.2 maximum_convert_fusion
  120.0 28.8 %reduce-scatter.3.cloned.1.call-done = bf16[16,12288]{1,0:T(8,128)(2,1)} async-done(((bf16[64,12288]{1,0:T(8,128)(2,1)}), bf16[16,12288]{1,0:T(8,128)(2,1)}) %reduce-scatter.3.cloned.1.call-update) | async-done | bytes 393232 | tf_op jit(solution)/shard_map/reduce_scatter | solution.py:86
  148.8 1.0 convert_bitcast_fusion.1
  149.8 0.2 copy.8
  150.0 3.8 %multiply_reduce_fusion.2 = (f32[16]{0:T(128)S(1)}, f32[16]{0:T(128)S(1)}, f32[16,4,24,128]{3,2,1,0:T(8,128)}) fusion(f32[16,4,24,128]{3,2,1,0:T(8,128)S(1)} %copy-done, f32[16,4,24,128]{3,2,1,0:T(8,128)S(1)} %bitcast.41, f32[16]{0:T(128)S(1)} %copy-done.2, f32[4,24,128]{2,1,0:T(8,128)} %param.5, f32[16,12,24,128]{3,2,1,0:T(8,128)S(1)} %maximum_convert_fusion), kind=kLoop, calls=%fused_computation.135 | loop fusion | flops 9043936 | bytes 11846272 | tf_op jit(solution)/shard_map/reduce_sum | solution.py:50
  153.8 13.4 %all-reduce.2 = (f32[16]{0:T(128)S(1)}, f32[16]{0:T(128)S(1)}) all-reduce(f32[16]{0:T(128)S(1)} %get-tuple-element.3, f32[16]{0:T(128)S(1)} %get-tuple-element.2), channel_id=1, replica_groups=mesh['grid'=8,'band'=4] {'grid'}, use_global_device_ids=true, to_apply=%region_1.0 | all-reduce | flops 32 | bytes 256 | tf_op jit(solution)/shard_map/psum | solution.py:70
  167.3 1.4 multiply_reduce_fusion.1
  168.7 11.8 %psum.45 = f32[16]{0:T(128)S(1)} all-reduce(f32[16]{0:T(128)S(1)} %multiply_reduce_fusion.1), channel_id=1, replica_groups=mesh['grid'=8,'band'=4] {'grid'}, use_global_device_ids=true, to_apply=%region_7.8 | all-reduce | flops 16 | bytes 128 | tf_op jit(solution)/shard_map/psum | solution.py:100
  180.5 2.3 fusion.86
  182.8 0.9 copy.31
  183.7 34.6 %all-gather.5.cloned.1.call-done = bf16[64,12288]{1,0:T(8,128)(2,1)} async-done(((bf16[16,12288]{1,0:T(8,128)(2,1)}), bf16[64,12288]{1,0:T(8,128)(2,1)}) %all-gather.5.cloned.1.call-update) | async-done | bytes 1572880 | tf_op jit(solution)/shard_map/all_gather | solution.py:80
  218.3 5.9 %fusion.10 = f32[256,64]{1,0:T(8,128)} fusion(bf16[64,12288]{1,0:T(8,128)(2,1)} %all-gather.5.cloned.1.call-done, bf16[32,8,96,128]{3,2,1,0:T(8,128)(2,1)} %bitcast.37), kind=kOutput, calls=%fused_computation.46 | convolution fusion | flops 402653184 | bytes 7929856 | tf_op jit(solution)/shard_map/dot_general | solution.py:78
  224.3 51.9 %all-reduce.8.cloned.1.call-done = f32[256,64]{1,0:T(8,128)} async-done(((f32[256,64]{1,0:T(8,128)}), f32[256,64]{1,0:T(8,128)}) %all-reduce.8.cloned.1.call-update) | async-done | bytes 65552 | tf_op jit(solution)/shard_map/psum | solution.py:84
  276.2 6.2 %convolution_convert_fusion = bf16[64,12288]{1,0:T(8,128)(2,1)} fusion(bf16[32,8,96,128]{3,2,1,0:T(8,128)(2,1)} %bitcast.38, f32[256,64]{1,0:T(8,128)} %all-reduce.8.cloned.1.call-done), kind=kOutput, calls=%fused_computation.32 | convolution fusion | flops 403472384 | bytes 7929856 | tf_op jit(solution)/shard_map/dot_general | solution.py:87
  282.4 1.3 collective-permute-start.3
  283.7 3.1 collective-permute-start.2
  286.7 1.3 collective-permute-done.2
  288.0 0.2 maximum_convert_fusion.1
  288.2 29.0 %reduce-scatter.5.cloned.1.call-done = bf16[16,12288]{1,0:T(8,128)(2,1)} async-done(((bf16[64,12288]{1,0:T(8,128)(2,1)}), bf16[16,12288]{1,0:T(8,128)(2,1)}) %reduce-scatter.5.cloned.1.call-update) | async-done | bytes 393232 | tf_op jit(solution)/shard_map/reduce_scatter | solution.py:86
  317.2 1.1 convert_bitcast_fusion
  318.5 3.9 %multiply_reduce_fusion = (f32[16]{0:T(128)S(1)}, f32[16,4,24,128]{3,2,1,0:T(8,128)}) fusion(f32[16,4,24,128]{3,2,1,0:T(8,128)S(1)} %copy-done.1, f32[16,4,24,128]{3,2,1,0:T(8,128)S(1)} %bitcast.42, f32[16]{0:T(128)S(1)} %copy-done.2, f32[4,24,128]{2,1,0:T(8,128)} %param.5, f32[16,12,24,128]{3,2,1,0:T(8,128)S(1)} %maximum_convert_fusion.1), kind=kLoop, calls=%fused_computation.131 | loop fusion | flops 8650736 | bytes 11846208 | tf_op jit(solution)/shard_map/reduce_sum | solution.py:50
  322.3 13.4 %psum.47 = f32[16]{0:T(128)S(1)} all-reduce(f32[16]{0:T(128)S(1)} %get-tuple-element.6), channel_id=1, replica_groups=mesh['grid'=8,'band'=4] {'grid'}, use_global_device_ids=true, to_apply=%region_11.12 | all-reduce | flops 16 | bytes 128 | tf_op jit(solution)/shard_map/psum | solution.py:95
  335.8 3.2 multiply_subtract_fusion
  (24 shorter events, 0.5 us)
Async XLA Ops:
  7.2 42.8 %all-gather.3.cloned.1.call-start = ((), (), s32[]{:S(2)}) async-start(), calls=%async_computation.2 | async-start | bytes 1966080 | tf_op jit(solution)/shard_map/all_gather | solution.py:80
  9.3 98.4 %all-reduce.6.cloned.1.call-start = ((), (), s32[]{:S(2)}) async-start(), calls=%async_computation.3 | async-start | bytes 262144 | tf_op jit(solution)/shard_map/psum | solution.py:84
  55.8 92.9 %reduce-scatter.3.cloned.1.call-start = ((), (), s32[]{:S(2)}) async-start(), calls=%async_computation.4 | async-start | bytes 1966080 | tf_op jit(solution)/shard_map/reduce_scatter | solution.py:86
  113.9 36.0 %copy-start = (f32[16,4,24,128]{3,2,1,0:T(8,128)S(1)}, f32[16,4,24,128]{3,2,1,0:T(8,128)}, u32[]{:S(2)}) copy-start(f32[16,4,24,128]{3,2,1,0:T(8,128)} %param.7) | copy-start | bytes 2359300
  114.0 36.0 %copy-start.2 = (f32[16]{0:T(128)S(1)}, f32[16]{0:T(128)}, u32[]{:S(2)}) copy-start(f32[16]{0:T(128)} %param.6) | copy-start | bytes 196
  114.0 104.4 %all-gather.5.cloned.1.call-start = ((), (), s32[]{:S(2)}) async-start(), calls=%async_computation.5 | async-start | bytes 1966080 | tf_op jit(solution)/shard_map/all_gather | solution.py:80
  114.0 4.5 %collective-permute-start.1 = (bf16[16,4,24,128]{3,2,1,0:T(8,128)(2,1)S(1)}, bf16[16,4,24,128]{3,2,1,0:T(8,128)(2,1)S(1)}, u32[]{:S(2)}, u32[]{:S(2)}) collective-permute-start(bf16[16,4,24,128]{3,2,1,0:T(8,128)(2,1)S(1)} %convert_element_type.31), channel_id=1, source_target_pairs={{4,0},{8,4},{12,8},{16,12},{20,16},{24,20},{28,24},{5,1},{9,5},{13... | collective-permute-start | bytes 1179656 | tf_op jit(solution)/shard_map/ppermute | solution.py:19
  115.5 4.4 %collective-permute-start = (bf16[16,4,24,128]{3,2,1,0:T(8,128)(2,1)S(1)}, bf16[16,4,24,128]{3,2,1,0:T(8,128)(2,1)S(1)}, u32[]{:S(2)}, u32[]{:S(2)}) collective-permute-start(bf16[16,4,24,128]{3,2,1,0:T(8,128)(2,1)S(1)} %convert_element_type.31), channel_id=1, source_target_pairs={{0,4},{4,8},{8,12},{12,16},{16,20},{20,24},{24,28},{1,5},{5,9},{9,... | collective-permute-start | bytes 1179656 | tf_op jit(solution)/shard_map/ppermute | solution.py:18
  183.7 92.5 %all-reduce.8.cloned.1.call-start = ((), (), s32[]{:S(2)}) async-start(), calls=%async_computation.6 | async-start | bytes 262144 | tf_op jit(solution)/shard_map/psum | solution.py:84
  224.2 93.0 %reduce-scatter.5.cloned.1.call-start = ((), (), s32[]{:S(2)}) async-start(), calls=%async_computation.7 | async-start | bytes 1966080 | tf_op jit(solution)/shard_map/reduce_scatter | solution.py:86
  282.4 4.4 %collective-permute-start.3 = (bf16[16,4,24,128]{3,2,1,0:T(8,128)(2,1)S(1)}, bf16[16,4,24,128]{3,2,1,0:T(8,128)(2,1)S(1)}, u32[]{:S(2)}, u32[]{:S(2)}) collective-permute-start(bf16[16,4,24,128]{3,2,1,0:T(8,128)(2,1)S(1)} %get-tuple-element.8), channel_id=1, source_target_pairs={{4,0},{8,4},{12,8},{16,12},{20,16},{24,20},{28,24},{5,1},{9,5},{13... | collective-permute-start | bytes 1179656 | tf_op jit(solution)/shard_map/ppermute | solution.py:19
  283.7 4.4 %collective-permute-start.2 = (bf16[16,4,24,128]{3,2,1,0:T(8,128)(2,1)S(1)}, bf16[16,4,24,128]{3,2,1,0:T(8,128)(2,1)S(1)}, u32[]{:S(2)}, u32[]{:S(2)}) collective-permute-start(bf16[16,4,24,128]{3,2,1,0:T(8,128)(2,1)S(1)} %get-tuple-element.8), channel_id=1, source_target_pairs={{0,4},{4,8},{8,12},{12,16},{16,20},{20,24},{24,28},{1,5},{5,9},{9,... | collective-permute-start | bytes 1179656 | tf_op jit(solution)/shard_map/ppermute | solution.py:18
  317.2 1.3 copy-start.1
Sparse Core Ops, SparseCore 0:
  10.1 39.7 all-gather.2
  56.0 51.7 all-reduce.5
  114.1 34.6 reduce-scatter.2
  183.8 34.4 all-gather.4
  224.4 51.7 all-reduce.7
  282.5 34.6 reduce-scatter.4
where the time goes:
time: 346 us
  waiting for transfers between devices  239 us (69%)
  blocking collectives  38.6 us (11%)
  matrix products  24 us (7%)
  other arithmetic  18.3 us (5%)
  between operations  14.2 us (4%)
  starting transfers between devices  9.07 us (3%)
    psum x2, waiting for transfers between devices, body(): margins = lax.psum(partial_margin, 'grid')  104 us
    all_gather x2, waiting for transfers between devices, body(): lax.all_gather(rounded, 'band', axis=0, tiled=True)  75.2 us
    reduce_scatter x2, waiting for transfers between devices, body(): lax.psum_scatter(lax.dot_general(scaled, occupied_rows, (((0,), (0,)), ((...  57.8 us
    psum x1, blocking collectives, body(): curvature = lax.psum(inner_product(direction, applied), 'grid')  13.4 us
    psum x1, blocking collectives, body(): norm_now = lax.psum(inner_product(source_term, source_term), 'grid')  13.4 us
    dot_general x2, matrix products, body(): lax.dot_general(scaled, occupied_rows, (((0,), (0,)), ((), ())), preferre...  12.3 us
    psum x1, blocking collectives, body(): norm_next = lax.psum(inner_product(residual, residual), 'grid')  11.8 us
    dot_general x2, matrix products, body(): lax.dot_general(occupied_rows, lax.all_gather(rounded, 'band', axis=0, ti...  11.7 us
  transfers between devices with their start and end apart: 10, of which 8 were waited for; matrix products, arithmetic and copies ran while one was open for 0% of the time, Pallas kernels for 0%

commit v1 on v0

--- a/solution.py
+++ b/solution.py
@@ -6,6 +6,22 @@
 
 ITERS = 2
 COEFFICIENTS = (-205.0 / 72.0, 8.0 / 5.0, -1.0 / 5.0, 8.0 / 315.0, -1.0 / 560.0)
+
+
+def ring_gather(x, axis, dim):
+    ways, here, step = (lax.axis_size(axis), lax.axis_index(axis), x.shape[dim])
+    shape = [n * ways if d == dim else n for d, n in enumerate(x.shape)]
+    full = lax.dynamic_update_slice_in_dim(jnp.zeros(shape, x.dtype), x, here * step, axis=dim)
+    going_up = going_down = x
+    for far in range(1, ways // 2 + 1):
+        going_up = lax.ppermute(going_up, axis, [(d, (d + 1) % ways) for d in range(ways)])
+        full = lax.dynamic_update_slice_in_dim(full, going_up, (here - far) % ways * step, axis=dim)
+        if 2 * far < ways:
+            going_down = lax.ppermute(going_down, axis, [(d, (d - 1) % ways) for d in range(ways)])
+            full = lax.dynamic_update_slice_in_dim(
+                full, going_down, (here + far) % ways * step, axis=dim
+            )
+    return full
 
 
 def with_halo(shard, sides, width):
@@ -77,7 +93,7 @@
         rounded = direction.astype(jnp.bfloat16).reshape(local_bands, local_cells)
         partial_margin = lax.dot_general(
             occupied_rows,
-            lax.all_gather(rounded, "band", axis=0, tiled=True),
+            ring_gather(rounded, "band", 0),
             (((1,), (1,)), ((), ())),
             preferred_element_type=jnp.float32,
         )

time: 346 us -> 324 us (0.936)
  waiting for transfers between devices: 239 us -> 207 us
  starting transfers between devices: 9.07 us -> 22.8 us
    all_gather x2 -> x0, waiting for transfers between devices: 75.2 us -> none  [body(): lax.all_gather(rounded, 'band', axis=0, tiled=True)]
    ppermute x0 -> x6, waiting for transfers between devices: none -> 46.3 us  [the longest x4 38.2 us: ring_gather(): lax.ppermute(going_up, axis, [(d, (d + 1) % ways) for d in range(ways)])]
    ppermute x0 -> x6, starting transfers between devices: none -> 13.7 us  [the longest x4 7.84 us: ring_gather(): lax.ppermute(going_up, axis, [(d, (d + 1) % ways) for d in range(ways)])]
  transfers between devices with their start and end apart: 10 -> 14, of which waited for: 8 -> 12; matrix products, arithmetic and copies ran while one was open for 0% -> 0% of each run, Pallas kernels for 0% -> 0%
where the time goes in v1:
time: 324 us; the launch traced here: 323 us
  waiting for transfers between devices  207 us (64%)
  blocking collectives  38.8 us (12%)
  matrix products  23.5 us (7%)
  starting transfers between devices  22.8 us (7%)
  other arithmetic  15.6 us (5%)
  between operations  14 us (4%)
    psum x2, waiting for transfers between devices, body(): margins = lax.psum(partial_margin, 'grid')  101 us
    reduce_scatter x2, waiting for transfers between devices, body(): lax.psum_scatter(lax.dot_general(scaled, occupied_rows, (((0,), (0,)), ((...  57.9 us
    ppermute x4, waiting for transfers between devices, ring_gather(): lax.ppermute(going_up, axis, [(d, (d + 1) % ways) for d in range(ways)])  38.2 us
    psum x1, blocking collectives, body(): norm_now = lax.psum(inner_product(source_term, source_term), 'grid')  13.6 us
    psum x1, blocking collectives, body(): curvature = lax.psum(inner_product(direction, applied), 'grid')  13.4 us
    dot_general x2, matrix products, body(): lax.dot_general(scaled, occupied_rows, (((0,), (0,)), ((), ())), preferre...  12.3 us
    psum x1, blocking collectives, body(): norm_next = lax.psum(inner_product(residual, residual), 'grid')  11.8 us
    dot_general x2, matrix products, body(): lax.dot_general(occupied_rows, ring_gather(rounded, 'band', 0), (((1,), (...  11.2 us
  transfers between devices with their start and end apart: 14, of which 12 were waited for; matrix products, arithmetic and copies ran while one was open for 0% of the time, Pallas kernels for 0%

profile of v1, /device:TPU:0, one launch (start us, length us, event | category | flops | bytes accessed | tf_op | source)
XLA Modules:
  0.0 323.5 jit_solution(13511933812761241231)
XLA Ops:
  7.2 1.2 convert_element_type.31
  8.6 3.1 collective-permute-start.2
  11.6 2.1 collective-permute-start.3
  14.0 9.6 %collective-permute-done.2 = bf16[16,12288]{1,0:T(8,128)(2,1)S(1)} collective-permute-done((bf16[16,12288]{1,0:T(8,128)(2,1)S(1)}, bf16[16,12288]{1,0:T(8,128)(2,1)S(1)}, u32[]{:S(2)}, u32[]{:S(2)}) %collective-permute-start.2) | collective-permute-done | bytes 393248 | tf_op jit(solution)/shard_map/ppermute | solution.py:17
  23.7 7.2 %collective-permute-done.3 = bf16[16,12288]{1,0:T(8,128)(2,1)S(1)} collective-permute-done((bf16[16,12288]{1,0:T(8,128)(2,1)S(1)}, bf16[16,12288]{1,0:T(8,128)(2,1)S(1)}, u32[]{:S(2)}, u32[]{:S(2)}) %collective-permute-start.3) | collective-permute-done | bytes 393248 | tf_op jit(solution)/shard_map/ppermute | solution.py:20
  30.9 8.8 %collective-permute-done.4 = bf16[16,12288]{1,0:T(8,128)(2,1)S(1)} collective-permute-done((bf16[16,12288]{1,0:T(8,128)(2,1)S(1)}, bf16[16,12288]{1,0:T(8,128)(2,1)S(1)}, u32[]{:S(2)}, u32[]{:S(2)}) %collective-permute-start.4) | collective-permute-done | bytes 393248 | tf_op jit(solution)/shard_map/ppermute | solution.py:17
  39.7 5.6 %fusion.10 = f32[256,64]{0,1:T(8,128)} fusion(bf16[64,12288]{1,0:T(8,128)(2,1)S(1)} %constant_dynamic-update-slice_fusion.4, bf16[32,8,96,128]{3,2,1,0:T(8,128)(2,1)} %bitcast.43), kind=kOutput, calls=%fused_computation.48 | convolution fusion | flops 402653184 | bytes 7929856 | tf_op jit(solution)/shard_map/dot_general | solution.py:94
  45.4 51.9 %all-reduce.6.cloned.1.call-done = f32[256,64]{0,1:T(8,128)} async-done(((f32[256,64]{0,1:T(8,128)}), f32[256,64]{0,1:T(8,128)}) %all-reduce.6.cloned.1.call-update) | async-done | bytes 65552 | tf_op jit(solution)/shard_map/psum | solution.py:100
  97.3 6.1 %convolution_convert_fusion.1 = bf16[64,12288]{1,0:T(8,128)(2,1)} fusion(bf16[32,8,96,128]{3,2,1,0:T(8,128)(2,1)} %bitcast.44, f32[256,64]{0,1:T(8,128)} %all-reduce.6.cloned.1.call-done), kind=kOutput, calls=%fused_computation.33 | convolution fusion | flops 403472384 | bytes 7929856 | tf_op jit(solution)/shard_map/dot_general | solution.py:103
  103.5 1.3 collective-permute-start.1
  104.8 3.1 collective-permute-start
  107.9 1.3 collective-permute-done
  109.4 28.9 %reduce-scatter.3.cloned.1.call-done = bf16[16,12288]{1,0:T(8,128)(2,1)} async-done(((bf16[64,12288]{1,0:T(8,128)(2,1)}), bf16[16,12288]{1,0:T(8,128)(2,1)}) %reduce-scatter.3.cloned.1.call-update) | async-done | bytes 393232 | tf_op jit(solution)/shard_map/reduce_scatter | solution.py:102
  139.5 3.0 multiply_reduce_fusion.2
  142.6 13.6 %all-reduce.2 = (f32[16]{0:T(128)S(1)}, f32[16]{0:T(128)S(1)}) all-reduce(f32[16]{0:T(128)S(1)} %get-tuple-element.3, f32[16]{0:T(128)S(1)} %get-tuple-element.2), channel_id=1, replica_groups=mesh['grid'=8,'band'=4] {'grid'}, use_global_device_ids=true, to_apply=%region_1.0 | all-reduce | flops 32 | bytes 256 | tf_op jit(solution)/shard_map/psum | solution.py:86
  156.1 1.4 multiply_reduce_fusion.1
  157.6 11.8 %psum.45 = f32[16]{0:T(128)S(1)} all-reduce(f32[16]{0:T(128)S(1)} %multiply_reduce_fusion.1), channel_id=1, replica_groups=mesh['grid'=8,'band'=4] {'grid'}, use_global_device_ids=true, to_apply=%region_7.8 | all-reduce | flops 16 | bytes 128 | tf_op jit(solution)/shard_map/psum | solution.py:116
  169.4 1.2 fusion.89
  170.8 3.8 %collective-permute-start.8 = (bf16[16,12288]{1,0:T(8,128)(2,1)S(1)}, bf16[16,12288]{1,0:T(8,128)(2,1)S(1)}, u32[]{:S(2)}, u32[]{:S(2)}) collective-permute-start(bf16[16,12288]{1,0:T(8,128)(2,1)S(1)} %bitcast.56), channel_id=1, source_target_pairs={{0,3},{1,0},{2,1},{3,2},{4,7},{5,4},{6,5},{7,6},{8,11},{9,8},{10,9... | collective-permute-start | bytes 1179656 | tf_op jit(solution)/shard_map/ppermute | solution.py:20
  174.8 9.7 %collective-permute-done.7 = bf16[16,12288]{1,0:T(8,128)(2,1)S(1)} collective-permute-done((bf16[16,12288]{1,0:T(8,128)(2,1)S(1)}, bf16[16,12288]{1,0:T(8,128)(2,1)S(1)}, u32[]{:S(2)}, u32[]{:S(2)}) %collective-permute-start.7) | collective-permute-done | bytes 393248 | tf_op jit(solution)/shard_map/ppermute | solution.py:17
  184.5 4.7 %collective-permute-start.9 = (bf16[16,12288]{1,0:T(8,128)(2,1)S(1)}, bf16[16,12288]{1,0:T(8,128)(2,1)S(1)}, u32[]{:S(2)}, u32[]{:S(2)}) collective-permute-start(bf16[16,12288]{1,0:T(8,128)(2,1)S(1)} %collective-permute-done.7), channel_id=1, source_target_pairs={{0,1},{1,2},{2,3},{3,0},{4,5},{5,6},{6,7},{7,4},{8,9},{9,10},{10,1... | collective-permute-start | bytes 1179656 | tf_op jit(solution)/shard_map/ppermute | solution.py:17
  190.2 10.1 %collective-permute-done.9 = bf16[16,12288]{1,0:T(8,128)(2,1)S(1)} collective-permute-done((bf16[16,12288]{1,0:T(8,128)(2,1)S(1)}, bf16[16,12288]{1,0:T(8,128)(2,1)S(1)}, u32[]{:S(2)}, u32[]{:S(2)}) %collective-permute-start.9) | collective-permute-done | bytes 393248 | tf_op jit(solution)/shard_map/ppermute | solution.py:17
  200.4 5.6 %fusion.13 = f32[256,64]{0,1:T(8,128)} fusion(bf16[64,12288]{1,0:T(8,128)(2,1)S(1)} %constant_dynamic-update-slice_fusion, bf16[32,8,96,128]{3,2,1,0:T(8,128)(2,1)} %bitcast.45), kind=kOutput, calls=%fused_computation.49 | convolution fusion | flops 402653184 | bytes 7929856 | tf_op jit(solution)/shard_map/dot_general | solution.py:94
  206.3 48.7 %all-reduce.8.cloned.1.call-done = f32[256,64]{0,1:T(8,128)} async-done(((f32[256,64]{0,1:T(8,128)}), f32[256,64]{0,1:T(8,128)}) %all-reduce.8.cloned.1.call-update) | async-done | bytes 65552 | tf_op jit(solution)/shard_map/psum | solution.py:100
  254.9 6.1 %convolution_convert_fusion = bf16[64,12288]{1,0:T(8,128)(2,1)} fusion(bf16[32,8,96,128]{3,2,1,0:T(8,128)(2,1)} %bitcast.46, f32[256,64]{0,1:T(8,128)} %all-reduce.8.cloned.1.call-done), kind=kOutput, calls=%fused_computation.32 | convolution fusion | flops 403472384 | bytes 7929856 | tf_op jit(solution)/shard_map/dot_general | solution.py:103
  261.1 1.3 collective-permute-start.6
  262.4 3.1 collective-permute-start.5
  265.5 1.3 collective-permute-done.5
  267.0 29.0 %reduce-scatter.5.cloned.1.call-done = bf16[16,12288]{1,0:T(8,128)(2,1)} async-done(((bf16[64,12288]{1,0:T(8,128)(2,1)}), bf16[16,12288]{1,0:T(8,128)(2,1)}) %reduce-scatter.5.cloned.1.call-update) | async-done | bytes 393232 | tf_op jit(solution)/shard_map/reduce_scatter | solution.py:102
  297.2 3.1 multiply_reduce_fusion
  300.3 13.4 %psum.47 = f32[16]{0:T(128)S(1)} all-reduce(f32[16]{0:T(128)S(1)} %get-tuple-element.6), channel_id=1, replica_groups=mesh['grid'=8,'band'=4] {'grid'}, use_global_device_ids=true, to_apply=%region_11.12 | all-reduce | flops 16 | bytes 128 | tf_op jit(solution)/shard_map/psum | solution.py:111
  313.8 3.2 multiply_subtract_fusion
  (46 shorter events, 5.2 us)
Async XLA Ops:
  7.2 90.1 %all-reduce.6.cloned.1.call-start = ((), (), s32[]{:S(2)}) async-start(), calls=%async_computation.2 | async-start | bytes 131072 | tf_op jit(solution)/shard_map/psum | solution.py:100
  8.6 15.1 %collective-permute-start.2 = (bf16[16,12288]{1,0:T(8,128)(2,1)S(1)}, bf16[16,12288]{1,0:T(8,128)(2,1)S(1)}, u32[]{:S(2)}, u32[]{:S(2)}) collective-permute-start(bf16[16,12288]{1,0:T(8,128)(2,1)S(1)} %bitcast.53), channel_id=1, source_target_pairs={{0,1},{1,2},{2,3},{3,0},{4,5},{5,6},{6,7},{7,4},{8,9},{9,10},{10,1... | collective-permute-start | bytes 1179656 | tf_op jit(solution)/shard_map/ppermute | solution.py:17
  11.6 19.2 %collective-permute-start.3 = (bf16[16,12288]{1,0:T(8,128)(2,1)S(1)}, bf16[16,12288]{1,0:T(8,128)(2,1)S(1)}, u32[]{:S(2)}, u32[]{:S(2)}) collective-permute-start(bf16[16,12288]{1,0:T(8,128)(2,1)S(1)} %bitcast.54), channel_id=1, source_target_pairs={{0,3},{1,0},{2,1},{3,2},{4,7},{5,4},{6,5},{7,6},{8,11},{9,8},{10,9... | collective-permute-start | bytes 1179656 | tf_op jit(solution)/shard_map/ppermute | solution.py:20
  23.7 16.0 %collective-permute-start.4 = (bf16[16,12288]{1,0:T(8,128)(2,1)S(1)}, bf16[16,12288]{1,0:T(8,128)(2,1)S(1)}, u32[]{:S(2)}, u32[]{:S(2)}) collective-permute-start(bf16[16,12288]{1,0:T(8,128)(2,1)S(1)} %collective-permute-done.2), channel_id=1, source_target_pairs={{0,1},{1,2},{2,3},{3,0},{4,5},{5,6},{6,7},{7,4},{8,9},{9,10},{10,1... | collective-permute-start | bytes 1179656 | tf_op jit(solution)/shard_map/ppermute | solution.py:17
  45.3 93.0 %reduce-scatter.3.cloned.1.call-start = ((), (), s32[]{:S(2)}) async-start(), calls=%async_computation.3 | async-start | bytes 1966080 | tf_op jit(solution)/shard_map/reduce_scatter | solution.py:102
  103.4 151.5 %all-reduce.8.cloned.1.call-start = ((), (), s32[]{:S(2)}) async-start(), calls=%async_computation.4 | async-start | bytes 131072 | tf_op jit(solution)/shard_map/psum | solution.py:100
  103.5 4.4 %collective-permute-start.1 = (bf16[16,4,24,128]{3,2,1,0:T(8,128)(2,1)S(1)}, bf16[16,4,24,128]{3,2,1,0:T(8,128)(2,1)S(1)}, u32[]{:S(2)}, u32[]{:S(2)}) collective-permute-start(bf16[16,4,24,128]{3,2,1,0:T(8,128)(2,1)S(1)} %convert_element_type.31), channel_id=1, source_target_pairs={{4,0},{8,4},{12,8},{16,12},{20,16},{24,20},{28,24},{5,1},{9,5},{13... | collective-permute-start | bytes 1179656 | tf_op jit(solution)/shard_map/ppermute | solution.py:35
  104.8 4.4 %collective-permute-start = (bf16[16,4,24,128]{3,2,1,0:T(8,128)(2,1)S(1)}, bf16[16,4,24,128]{3,2,1,0:T(8,128)(2,1)S(1)}, u32[]{:S(2)}, u32[]{:S(2)}) collective-permute-start(bf16[16,4,24,128]{3,2,1,0:T(8,128)(2,1)S(1)} %convert_element_type.31), channel_id=1, source_target_pairs={{0,4},{4,8},{8,12},{12,16},{16,20},{20,24},{24,28},{1,5},{5,9},{9,... | collective-permute-start | bytes 1179656 | tf_op jit(solution)/shard_map/ppermute | solution.py:34
  109.3 30.2 %copy-start = (f32[16,4,24,128]{3,2,1,0:T(8,128)S(1)}, f32[16,4,24,128]{3,2,1,0:T(8,128)}, u32[]{:S(2)}) copy-start(f32[16,4,24,128]{3,2,1,0:T(8,128)} %param.7) | copy-start | bytes 2359300
  109.3 30.2 %copy-start.3 = (f32[4,24,128]{2,1,0:T(8,128)S(1)}, f32[4,24,128]{2,1,0:T(8,128)}, u32[]{:S(2)}) copy-start(f32[4,24,128]{2,1,0:T(8,128)} %param.5) | copy-start | bytes 147460
  109.4 30.2 %copy-start.5 = (f32[16]{0:T(128)S(1)}, f32[16]{0:T(128)}, u32[]{:S(2)}) copy-start(f32[16]{0:T(128)} %param.6) | copy-start | bytes 196
  142.6 26.8 %copy-start.1 = (f32[16,4,24,128]{3,2,1,0:T(8,128)S(1)}, f32[16,4,24,128]{3,2,1,0:T(8,128)}, u32[]{:S(2)}) copy-start(f32[16,4,24,128]{3,2,1,0:T(8,128)} %get-tuple-element.10) | copy-start | bytes 2359300
  170.7 13.8 %collective-permute-start.7 = (bf16[16,12288]{1,0:T(8,128)(2,1)S(1)}, bf16[16,12288]{1,0:T(8,128)(2,1)S(1)}, u32[]{:S(2)}, u32[]{:S(2)}) collective-permute-start(bf16[16,12288]{1,0:T(8,128)(2,1)S(1)} %bitcast.55), channel_id=1, source_target_pairs={{0,1},{1,2},{2,3},{3,0},{4,5},{5,6},{6,7},{7,4},{8,9},{9,10},{10,1... | collective-permute-start | bytes 1179656 | tf_op jit(solution)/shard_map/ppermute | solution.py:17
  170.8 19.4 %collective-permute-start.8 = (bf16[16,12288]{1,0:T(8,128)(2,1)S(1)}, bf16[16,12288]{1,0:T(8,128)(2,1)S(1)}, u32[]{:S(2)}, u32[]{:S(2)}) collective-permute-start(bf16[16,12288]{1,0:T(8,128)(2,1)S(1)} %bitcast.56), channel_id=1, source_target_pairs={{0,3},{1,0},{2,1},{3,2},{4,7},{5,4},{6,5},{7,6},{8,11},{9,8},{10,9... | collective-permute-start | bytes 1179656 | tf_op jit(solution)/shard_map/ppermute | solution.py:20
  184.5 15.8 %collective-permute-start.9 = (bf16[16,12288]{1,0:T(8,128)(2,1)S(1)}, bf16[16,12288]{1,0:T(8,128)(2,1)S(1)}, u32[]{:S(2)}, u32[]{:S(2)}) collective-permute-start(bf16[16,12288]{1,0:T(8,128)(2,1)S(1)} %collective-permute-done.7), channel_id=1, source_target_pairs={{0,1},{1,2},{2,3},{3,0},{4,5},{5,6},{6,7},{7,4},{8,9},{9,10},{10,1... | collective-permute-start | bytes 1179656 | tf_op jit(solution)/shard_map/ppermute | solution.py:17
  206.0 89.9 %reduce-scatter.5.cloned.1.call-start = ((), (), s32[]{:S(2)}) async-start(), calls=%async_computation.5 | async-start | bytes 1966080 | tf_op jit(solution)/shard_map/reduce_scatter | solution.py:102
  261.1 4.4 %collective-permute-start.6 = (bf16[16,4,24,128]{3,2,1,0:T(8,128)(2,1)S(1)}, bf16[16,4,24,128]{3,2,1,0:T(8,128)(2,1)S(1)}, u32[]{:S(2)}, u32[]{:S(2)}) collective-permute-start(bf16[16,4,24,128]{3,2,1,0:T(8,128)(2,1)S(1)} %get-tuple-element.8), channel_id=1, source_target_pairs={{4,0},{8,4},{12,8},{16,12},{20,16},{24,20},{28,24},{5,1},{9,5},{13... | collective-permute-start | bytes 1179656 | tf_op jit(solution)/shard_map/ppermute | solution.py:35
  262.4 4.4 %collective-permute-start.5 = (bf16[16,4,24,128]{3,2,1,0:T(8,128)(2,1)S(1)}, bf16[16,4,24,128]{3,2,1,0:T(8,128)(2,1)S(1)}, u32[]{:S(2)}, u32[]{:S(2)}) collective-permute-start(bf16[16,4,24,128]{3,2,1,0:T(8,128)(2,1)S(1)} %get-tuple-element.8), channel_id=1, source_target_pairs={{0,4},{4,8},{8,12},{12,16},{16,20},{20,24},{24,28},{1,5},{5,9},{9,... | collective-permute-start | bytes 1179656 | tf_op jit(solution)/shard_map/ppermute | solution.py:34
  267.0 30.3 %copy-start.4 = (f32[4,24,128]{2,1,0:T(8,128)S(1)}, f32[4,24,128]{2,1,0:T(8,128)}, u32[]{:S(2)}) copy-start(f32[4,24,128]{2,1,0:T(8,128)} %param.5) | copy-start | bytes 147460
  295.9 1.3 copy-start.2
Sparse Core Ops, SparseCore 0:
  45.4 51.7 all-reduce.5
  103.6 34.6 reduce-scatter.2
  206.1 48.7 all-reduce.7
  261.2 34.6 reduce-scatter.4
